TPU v7x, 32 devices: a whole 2x2x4 slice. The times are simulated.
32 devices in a mesh: seq: 8 (over z, y), fsdp: 4 (over x, core).
Axes of the slice: x: 2, y: 2, z: 4, core: 2. Of those that a mesh axis runs over, the one named last changes fastest.
Arguments:
- inputs: bfloat16 [12288, 1536], P(('seq', 'fsdp')), may hold values from -15 to 15
- layer_norm_gain: float32 [1536], replicated, may hold values from 0.25 to 1.75
- layer_norm_bias: float32 [1536], replicated, may hold values from -4 to 4
- w_in: bfloat16 [1536, 3072], P('fsdp'), may hold values from -0.15625 to 0.15625
- dw_kernel: float32 [32, 1536], replicated, may hold values from -1 to 1
- bn_gain: float32 [1536], replicated, may hold values from 0.25 to 1.75
- bn_bias: float32 [1536], replicated, may hold values from -4 to 4
- cotangent: bfloat16 [12288, 1536], P(('seq', 'fsdp')), may hold values from -6 to 6
Outputs:
- output: bfloat16 [12288, 1536], P(('seq', 'fsdp'))
- input_gradient: bfloat16 [12288, 1536], P(('seq', 'fsdp'))
- grad_w_in: float32 [1536, 3072], P('fsdp')
- grad_kernel: float32 [32, 1536], replicated
- grad_bn_gain: float32 [1536], replicated
- grad_bn_bias: float32 [1536], replicated
- layer_norm_gain_gradient: float32 [1536], replicated
- grad_ln_bias: float32 [1536], replicated
All inputs are finite; a program needn't handle non-finite values.
Results may differ from a plain program's by a relative error of at most 0.012.
The roundings to bfloat16 on the way count: a program that leaves them out, or rounds other values in their place, can miss the bound.
Values may be sent and summed in bfloat16 or wider, within the bound.
No kernel may reach another device: no remote copies, remote signals or barrier semaphores. Data moves between devices by JAX's collectives and lax.ppermute only.
A program may use at most 128 MiB of HBM per device.

v0:
```python
import jax
import jax.numpy as jnp
from jax import lax
from jax.sharding import PartitionSpec as P

epsilon = 1e-05


def from_behind(block, axis, distance):
    devices = range(lax.axis_size(axis))
    route = [(i - distance, i) for i in devices if i - distance in devices]
    return lax.ppermute(block, axis, route)


def on_device(
    inputs, layer_norm_gain, layer_norm_bias, w_in, dw_kernel, bn_gain, bn_bias, cotangent
):
    tok_rows = inputs.shape[0]
    features = inputs.shape[1]
    kernel_len = dw_kernel.shape[0]
    all_frames = tok_rows * lax.axis_size("seq") * lax.axis_size("fsdp")
    frames = inputs.astype(jnp.float32)
    row_mean = jnp.mean(frames, axis=-1, keepdims=True)
    centered_rows = frames - row_mean
    row_inverse_deviation = lax.rsqrt(
        jnp.mean(centered_rows * centered_rows, axis=-1, keepdims=True) + epsilon
    )
    standardized_input = centered_rows * row_inverse_deviation
    normalized_rows = (standardized_input * layer_norm_gain + layer_norm_bias).astype(jnp.bfloat16)
    full_weight = lax.all_gather(w_in, "fsdp", axis=0, tiled=True)
    hidden = jnp.dot(normalized_rows, full_weight, preferred_element_type=jnp.float32)
    value_part = hidden[:, :features]
    gate_sig = jax.nn.sigmoid(hidden[:, features:])
    glu = (value_part * gate_sig).astype(jnp.bfloat16)
    past_rim = from_behind(glu[tok_rows - (kernel_len - 1) :], ("seq", "fsdp"), 1)
    padded_glu = jnp.concatenate([past_rim, glu], axis=0).astype(jnp.float32)
    conv_out = jnp.zeros((tok_rows, features), jnp.float32)
    for offset in range(kernel_len):
        conv_out = (
            conv_out
            + dw_kernel[offset]
            * padded_glu[kernel_len - 1 - offset : kernel_len - 1 - offset + tok_rows]
        )
    chan_mean = lax.psum(jnp.sum(conv_out, axis=0), ("seq", "fsdp")) / all_frames
    conv_centred = conv_out - chan_mean
    chan_var = lax.psum(jnp.sum(conv_centred * conv_centred, axis=0), ("seq", "fsdp")) / all_frames
    bn_rstd = lax.rsqrt(chan_var + epsilon)
    chat = conv_centred * bn_rstd
    z_value = chat * bn_gain + bn_bias
    z_sig = jax.nn.sigmoid(z_value)
    output = (z_value * z_sig).astype(jnp.bfloat16)
    grad_z = cotangent.astype(jnp.float32) * z_sig * (1.0 + z_value * (1.0 - z_sig))
    grad_bn_bias, grad_bn_gain = lax.psum(
        (jnp.sum(grad_z, axis=0), jnp.sum(grad_z * chat, axis=0)), ("seq", "fsdp")
    )
    grad_conv = (
        bn_gain * bn_rstd * (grad_z - grad_bn_bias / all_frames - chat * grad_bn_gain / all_frames)
    )
    future_rim = from_behind(grad_conv[: kernel_len - 1], ("seq", "fsdp"), -1)
    padded_grad = jnp.concatenate([grad_conv, future_rim], axis=0)
    grad_glu = jnp.zeros((tok_rows, features), jnp.float32)
    kernel_rows = []
    for offset in range(kernel_len):
        grad_glu = grad_glu + dw_kernel[offset] * padded_grad[offset : offset + tok_rows]
        kernel_rows.append(
            jnp.sum(
                grad_conv
                * padded_glu[kernel_len - 1 - offset : kernel_len - 1 - offset + tok_rows],
                axis=0,
            )
        )
    kernel_portion = jnp.stack(kernel_rows, axis=0)
    grad_value = grad_glu * gate_sig
    grad_gate = grad_glu * value_part * gate_sig * (1.0 - gate_sig)
    grad_hidden = jnp.concatenate([grad_value, grad_gate], axis=1).astype(jnp.bfloat16)
    normalized_gradient = lax.dot_general(
        grad_hidden, full_weight, (((1,), (1,)), ((), ())), preferred_element_type=jnp.float32
    )
    grad_kernel, layer_norm_gain_gradient, grad_ln_bias = lax.psum(
        (
            kernel_portion,
            jnp.sum(normalized_gradient * standardized_input, axis=0),
            jnp.sum(normalized_gradient, axis=0),
        ),
        ("seq", "fsdp"),
    )
    rescaled_rows = normalized_gradient * layer_norm_gain
    input_gradient = row_inverse_deviation * (
        rescaled_rows
        - jnp.mean(rescaled_rows, axis=-1, keepdims=True)
        - standardized_input * jnp.mean(rescaled_rows * standardized_input, axis=-1, keepdims=True)
    )
    row_share = lax.psum_scatter(
        lax.dot_general(
            normalized_rows,
            grad_hidden,
            (((0,), (0,)), ((), ())),
            preferred_element_type=jnp.float32,
        ),
        "fsdp",
        scatter_dimension=0,
        tiled=True,
    )
    grad_w_in = lax.psum(row_share, "seq")
    return (
        output,
        input_gradient.astype(jnp.bfloat16),
        grad_w_in,
        grad_kernel,
        grad_bn_gain,
        grad_bn_bias,
        layer_norm_gain_gradient,
        grad_ln_bias,
    )


def solution(mesh):
    placed = (
        P(("seq", "fsdp"), None),
        P(),
        P(),
        P("fsdp", None),
        P(),
        P(),
        P(),
        P(("seq", "fsdp"), None),
    )
    return jax.shard_map(
        on_device,
        mesh=mesh,
        in_specs=placed,
        out_specs=(
            P(("seq", "fsdp"), None),
            P(("seq", "fsdp"), None),
            P("fsdp", None),
            P(),
            P(),
            P(),
            P(),
            P(),
        ),
        check_vma=False,
    )
```

profile of v0, /device:TPU:0, one launch (start us, length us, event | category | flops | bytes accessed | tf_op | source)
XLA Modules:
  0.0 759.2 jit_solution(17330102155597915595)
XLA Ops:
  9.3 67.3 %all-gather.2.cloned.1.call-done = bf16[1536,3072]{1,0:T(8,128)(2,1)} async-done(((bf16[384,3072]{1,0:T(8,128)(2,1)}), bf16[1536,3072]{1,0:T(8,128)(2,1)}) %all-gather.2.cloned.1.call-update) | async-done | bytes 9437200 | tf_op jit(solution)/shard_map/all_gather | solution.py:30
  76.6 6.7 fusion.115
  83.9 1.5 copy-done
  85.5 2.2 collective-permute-start
  88.9 10.2 %fusion.119 = (f32[1536]{0:T(1024)S(1)}, f32[384,1536]{1,0:T(8,128)}) fusion(f32[415,1536]{1,0:T(8,128)S(1)} %maximum_convert_fusion, f32[1536]{0:T(1024)S(1)} %get-tuple-element.76, f32[1536]{0:T(1024)S(1)} %get-tuple-element.77, f32[1536]{0:T(1024)S(1)} %get-tuple-element.47, f32[1536]{0:T(1024)S(1)} %get-tuple-element.48, ...), kind=kLoop, calls=%fused_computation.261 | loop fusion | flops 37747200 | bytes 78059520 | tf_op jit(solution)/shard_map/reduce_sum | solution.py:44
  99.1 44.0 %psum.56 = f32[1536]{0:T(1024)S(1)} all-reduce(f32[1536]{0:T(1024)S(1)} %get-tuple-element.85), channel_id=1, replica_groups=mesh['seq'=8,'fsdp'=4] {'seq','fsdp'}, use_global_device_ids=true, to_apply=%region_3.0 | all-reduce | flops 1536 | bytes 12288 | tf_op jit(solution)/shard_map/psum | solution.py:44
  143.2 1.9 multiply_reduce_fusion.33
  145.1 40.1 %psum.57 = f32[1536]{0:T(1024)S(1)} all-reduce(f32[1536]{0:T(1024)S(1)} %multiply_reduce_fusion.33), channel_id=1, replica_groups=mesh['seq'=8,'fsdp'=4] {'seq','fsdp'}, use_global_device_ids=true, to_apply=%region_5.0 | all-reduce | flops 1536 | bytes 12288 | tf_op jit(solution)/shard_map/psum | solution.py:46
  185.3 4.5 fusion.117
  189.7 40.2 %all-reduce.1 = (f32[1536]{0:T(1024)S(1)}, f32[1536]{0:T(1024)S(1)}) all-reduce(f32[1536]{0:T(1024)S(1)} %get-tuple-element.41, f32[1536]{0:T(1024)S(1)} %get-tuple-element.40), channel_id=1, replica_groups=mesh['seq'=8,'fsdp'=4] {'seq','fsdp'}, use_global_device_ids=true, to_apply=%region_9.0 | all-reduce | flops 3072 | bytes 24576 | tf_op jit(solution)/shard_map/psum | solution.py:53
  230.5 8.2 %multiply_reduce_fusion = (f32[1536]{0:T(1024)S(1)}, f32[1536]{0:T(1024)S(1)}, f32[1536]{0:T(1024)S(1)}, f32[1536]{0:T(1024)S(1)}, f32[1536]{0:T(1024)S(1)}, /*i...) fusion(f32[415,1536]{1,0:T(8,128)S(1)} %maximum_convert_fusion,, ...), kind=kLoop, calls=%fused_computation.169 | loop fusion | flops 31822848 | bytes 48519168 | tf_op jit(solution)/shard_map/reduce_sum | solution.py:66
  241.7 1.9 collective-permute-done.1
  243.5 40.4 %multiply_convert_fusion.1 = (bf16[384,1536]{1,0:T(8,128)(2,1)S(1)}, f32[384,1536]{1,0:T(8,128)}) fusion(f32[384,3072]{1,0:T(8,128)} %copy-done, f32[31,1536]{1,0:T(8,128)S(1)} %collective-permute-done.1, f32[384,1536]{1,0:T(8,128)} %copy-done.1, f32[1536]{0:T(1024)S(1)} %get-tuple-element.76, f32[1536]{0:T(1024)S(1)} %get-tuple-element.77, ...), kind=kLoop, calls=%fused_computation.202 | loop fusion | flops 58392576 | bytes 8644608 | tf_op jit(solution)/shard_map/convert
  284.0 4.4 multiply_convert_fusion
  289.4 9.4 %fusion.109 = f32[1536,3072]{1,0:T(8,128)} fusion(bf16[384,1536]{1,0:T(8,128)(2,1)S(1)} %multiply_convert_fusion, bf16[384,1536]{1,0:T(8,128)(2,1)S(1)} %get-tuple-element.83, bf16[384,1536]{1,0:T(8,128)(2,1)S(1)} %copy-done.3, f32[1536]{0:T(1024)S(1)} %copy-done.12, f32[1536]{0:T(1024)S(1)} %copy-done.11, f32[384]{0:T(512)S(1)} %add_rsqrt_fusion.1, ...), kind=kOutput, calls=%fused_computation.214 | convolution fusion | flops 3632136192 | bytes 22428672 | tf_op jit(solution)/shard_map/dot_general | solution.py:94
  298.9 5.4 multiply_reduce_fusion.18
  304.8 2.8 stack.131
  307.9 134.5 %reduce-scatter.2.cloned.1.call-done = f32[384,3072]{1,0:T(8,128)} async-done(((f32[1536,3072]{1,0:T(8,128)}), f32[384,3072]{1,0:T(8,128)}) %reduce-scatter.2.cloned.1.call-update) | async-done | bytes 4718608 | tf_op jit(solution)/shard_map/reduce_scatter | solution.py:93
  444.3 10.0 %fusion.12 = (f32[1536]{0:T(1024)}, f32[384]{0:T(512)}, f32[384]{0:T(512)}, f32[1536]{0:T(1024)}, f32[384,1536]{1,0:T(8,128)}) fusion(bf16[384,1536]{1,0:T(8,128)(2,1)S(1)} %copy-done.4, f32[384]{0:T(512)S(1)} %add_rsqrt_fusion.1, f32[384]{0:T(512)S(1)} %broadcast_multiply_fusion.4, f32[1536]{0:T(1024)S(1)} %copy-done.11, ...), kind=kOutput, calls=%fused_computation.44 | convolution fusion | flops 3634491392 | bytes 15360000 | tf_op jit(solution)/shard_map/dot_general | solution.py:76
  454.3 39.7 %all-reduce = (f32[1536]{0:T(1024)}, f32[1536]{0:T(1024)}) all-reduce(f32[1536]{0:T(1024)} %get-tuple-element.42, f32[1536]{0:T(1024)} %get-tuple-element.45), channel_id=1, replica_groups=mesh['seq'=8,'fsdp'=4] {'seq','fsdp'}, use_global_device_ids=true, to_apply=%region_48.0 | all-reduce | flops 3072 | bytes 24576 | tf_op jit(solution)/shard_map/psum | solution.py:79
  494.7 3.4 fusion.11
  498.1 74.3 %all-reduce.7.cloned.1.call-done = f32[32,1536]{1,0:T(8,128)} async-done(((f32[32,1536]{1,0:T(8,128)}), f32[32,1536]{1,0:T(8,128)}) %all-reduce.7.cloned.1.call-update) | async-done | bytes 196624 | tf_op jit(solution)/shard_map/psum | solution.py:79
  572.4 174.5 %all-reduce.5.cloned.1.call-done = f32[384,3072]{1,0:T(8,128)} async-done(((f32[384,3072]{1,0:T(8,128)}), f32[384,3072]{1,0:T(8,128)}) %all-reduce.5.cloned.1.call-update) | async-done | bytes 4718608 | tf_op jit(solution)/shard_map/psum | solution.py:104
  746.9 5.1 copy.18
  (90 shorter events, 12.3 us)
Async XLA Ops:
  7.2 0.9 copy-start.10
  7.2 1.4 copy-start.2
  7.2 69.4 %copy-start.11 = (f32[1536]{0:T(1024)S(1)}, f32[1536]{0:T(1024)}, u32[]{:S(2)}) copy-start(f32[1536]{0:T(1024)} %param.9) | copy-start | bytes 18436
  7.2 69.4 %copy-start.12 = (f32[1536]{0:T(1024)S(1)}, f32[1536]{0:T(1024)}, u32[]{:S(2)}) copy-start(f32[1536]{0:T(1024)} %param.10) | copy-start | bytes 18436
  7.2 69.4 %all-gather.2.cloned.1.call-start = ((), (), s32[]{:S(2)}) async-start(), calls=%async_computation.1 | async-start | bytes 11796480 | tf_op jit(solution)/shard_map/all_gather | solution.py:30
  7.9 434.4 %reduce-scatter.2.cloned.1.call-start = ((), (), s32[]{:S(2)}) async-start(), calls=%async_computation.2 | async-start | bytes 23592960 | tf_op jit(solution)/shard_map/reduce_scatter | solution.py:93
  83.2 2.2 copy-start
  85.5 3.1 collective-permute-start
  99.1 86.1 %copy-start.13 = (f32[1536]{0:T(1024)S(1)}, f32[1536]{0:T(1024)}, u32[]{:S(2)}) copy-start(f32[1536]{0:T(1024)} %param.13) | copy-start | bytes 18436
  99.1 86.1 %copy-start.14 = (f32[1536]{0:T(1024)S(1)}, f32[1536]{0:T(1024)}, u32[]{:S(2)}) copy-start(f32[1536]{0:T(1024)} %param.14) | copy-start | bytes 18436
  229.9 0.6 copy-start.16
  229.9 8.9 %copy-start.15 = (f32[1536]{0:T(1024)}, f32[1536]{0:T(1024)S(1)}, u32[]{:S(2)}) copy-start(f32[1536]{0:T(1024)S(1)} %get-tuple-element.97) | copy-start | bytes 18436
  238.8 1.4 copy-start.1
  240.2 3.3 collective-permute-start.1
  283.9 4.5 copy-start.5
  283.9 5.5 copy-start.3
  288.4 1.0 copy-start.7
  298.8 273.6 %all-reduce.7.cloned.1.call-start = ((), (), s32[]{:S(2)}) async-start(), calls=%async_computation.4 | async-start | bytes 393216 | tf_op jit(solution)/shard_map/psum | solution.py:79
  307.6 439.3 %all-reduce.5.cloned.1.call-start = ((), (), s32[]{:S(2)}) async-start(), calls=%async_computation.3 | async-start | bytes 9437184 | tf_op jit(solution)/shard_map/psum | solution.py:104
  442.4 1.3 copy-start.4
  442.4 1.6 copy-start.6
  442.4 2.0 copy-start.8
  746.9 5.1 copy-start.9
Sparse Core Ops, SparseCore 0:
  9.6 66.9 all-gather.1
  298.9 143.3 reduce-scatter.1
  449.4 122.9 all-reduce.6
  576.3 170.5 all-reduce.4
where the time goes:
time: 760 us; the launch traced here: 759 us
  waiting for transfers between devices  454 us (60%)
  blocking collectives  164 us (22%)
  other arithmetic  80.9 us (11%)
  matrix products  26 us (3%)
  local copies, waits for them, and re-layouts  16.1 us (2%)
  between operations  14.2 us (2%)
    psum x1, waiting for transfers between devices, on_device(): grad_w_in = lax.psum(row_share, 'seq')  174 us
    reduce_scatter x1, waiting for transfers between devices, on_device(): lax.psum_scatter(lax.dot_general(normalized_rows, grad_hidden, (((0,), (0...  135 us
    psum x1, waiting for transfers between devices, on_device(): lax.psum((kernel_portion, jnp.sum(normalized_gradient * standardized_inpu...  74.3 us
    all_gather x1, waiting for transfers between devices, on_device(): full_weight = lax.all_gather(w_in, 'fsdp', axis=0, tiled=True)  67.3 us
    another operation x2, other arithmetic  44.8 us
    psum x1, blocking collectives, on_device(): lax.psum(jnp.sum(conv_out, axis=0), ('seq', 'fsdp')) / all_frames  44 us
    psum x1, blocking collectives, on_device(): lax.psum((jnp.sum(grad_z, axis=0), jnp.sum(grad_z * chat, axis=0)), ('seq...  40.2 us
    psum x1, blocking collectives, on_device(): lax.psum(jnp.sum(conv_centred * conv_centred, axis=0), ('seq', 'fsdp'))  40.1 us
  transfers between devices with their start and end apart: 6, of which 6 were waited for; matrix products, arithmetic and copies ran while one was open for 3% of the time, Pallas kernels for 0%

commit v1 on v0

--- a/solution.py
+++ b/solution.py
@@ -27,7 +27,14 @@
     )
     standardized_input = centered_rows * row_inverse_deviation
     normalized_rows = (standardized_input * layer_norm_gain + layer_norm_bias).astype(jnp.bfloat16)
-    full_weight = lax.all_gather(w_in, "fsdp", axis=0, tiled=True)
+    ways, here = (lax.axis_size("fsdp"), lax.axis_index("fsdp"))
+    full_weight, reach = (w_in, 1)
+    while reach < ways:
+        theirs = lax.ppermute(full_weight, "fsdp", [(d, d ^ reach) for d in range(ways)])
+        mine_first = jnp.concatenate([full_weight, theirs], axis=0)
+        theirs_first = jnp.concatenate([theirs, full_weight], axis=0)
+        full_weight = jnp.where(here & reach == 0, mine_first, theirs_first)
+        reach = 2 * reach
     hidden = jnp.dot(normalized_rows, full_weight, preferred_element_type=jnp.float32)
     value_part = hidden[:, :features]
     gate_sig = jax.nn.sigmoid(hidden[:, features:])

time: 760 us -> 735 us (0.967)
  waiting for transfers between devices: 454 us -> 407 us
  other arithmetic: 80.9 us -> 89.6 us
    ppermute x0 -> x2, waiting for transfers between devices: none -> 104 us  [on_device(): lax.ppermute(full_weight, 'fsdp', [(d, d ^ reach) for d in range(ways)])]
    psum x1, waiting for transfers between devices: 74.3 us -> 0.01 us  [on_device(): lax.psum((kernel_portion, jnp.sum(normalized_gradient * standardized_inpu...]
    all_gather x1 -> x0, waiting for transfers between devices: 67.3 us -> none  [on_device(): full_weight = lax.all_gather(w_in, 'fsdp', axis=0, tiled=True)]
    psum x1, waiting for transfers between devices: 174 us -> 166 us  [on_device(): grad_w_in = lax.psum(row_share, 'seq')]
  transfers between devices with their start and end apart: 6 -> 7, of which waited for: 6 -> 5; matrix products, arithmetic and copies ran while one was open for 3% -> 4% of each run, Pallas kernels for 0% -> 0%
where the time goes in v1:
time: 735 us; the launch traced here: 734 us
  waiting for transfers between devices  407 us (55%)
  blocking collectives  164 us (22%)
  other arithmetic  89.6 us (12%)
  matrix products  31.6 us (4%)
  local copies, waits for them, and re-layouts  18.9 us (3%)
  between operations  15.9 us (2%)
    psum x1, waiting for transfers between devices, on_device(): grad_w_in = lax.psum(row_share, 'seq')  166 us
    reduce_scatter x1, waiting for transfers between devices, on_device(): lax.psum_scatter(lax.dot_general(normalized_rows, grad_hidden, (((0,), (0...  135 us
    ppermute x2, waiting for transfers between devices, on_device(): lax.ppermute(full_weight, 'fsdp', [(d, d ^ reach) for d in range(ways)])  104 us
    another operation x2, other arithmetic  46.8 us
    psum x1, blocking collectives, on_device(): lax.psum(jnp.sum(conv_out, axis=0), ('seq', 'fsdp')) / all_frames  44.4 us
    psum x1, blocking collectives, on_device(): lax.psum(jnp.sum(conv_centred * conv_centred, axis=0), ('seq', 'fsdp'))  40.4 us
    psum x1, blocking collectives, on_device(): lax.psum((jnp.sum(grad_z, axis=0), jnp.sum(grad_z * chat, axis=0)), ('seq...  40 us
    psum x1, blocking collectives, on_device(): lax.psum((kernel_portion, jnp.sum(normalized_gradient * standardized_inpu...  39.6 us
  transfers between devices with their start and end apart: 7, of which 5 were waited for; matrix products, arithmetic and copies ran while one was open for 4% of the time, Pallas kernels for 0%

profile of v1, /device:TPU:0, one launch (start us, length us, event | category | flops | bytes accessed | tf_op | source)
XLA Modules:
  0.0 734.2 jit_solution(17657199473934419323)
XLA Ops:
  8.6 4.4 collective-permute-done
  12.9 6.7 maximum_select_fusion.1
  19.6 2.9 collective-permute-start.1
  22.5 2.0 slice_reduce_fusion.31
  25.2 99.7 %collective-permute-done.1 = bf16[768,3072]{1,0:T(8,128)(2,1)} collective-permute-done((bf16[768,3072]{1,0:T(8,128)(2,1)}, bf16[768,3072]{1,0:T(8,128)(2,1)}, u32[]{:S(2)}, u32[]{:S(2)}) %collective-permute-start.1) | collective-permute-done | bytes 4718624 | tf_op jit(solution)/shard_map/ppermute | solution.py:33
  124.9 9.6 %fusion.110 = f32[384,3072]{1,0:T(8,128)S(1)} fusion(bf16[768,3072]{1,0:T(8,128)(2,1)} %collective-permute-done.1, bf16[768,3072]{1,0:T(8,128)(2,1)} %maximum_select_fusion.1, pred[]{:T(512)S(6)} %eq.6, bf16[384,1536]{1,0:T(8,128)(2,1)S(1)} %copy-done.2, f32[1536]{0:T(1024)S(1)} %copy-done.11, f32[1536]{0:T(1024)S(1)} %copy-done.10, ...), kind=kOutput, calls=%fused_computation.217 | convolution fusion | flops 3669884928 | bytes 15350785 | tf_op jit(solution)/shard_map/dot_general | solution.py:38
  140.2 10.2 %fusion.120 = (f32[1536]{0:T(1024)S(1)}, f32[384,1536]{1,0:T(8,128)}) fusion(f32[415,1536]{1,0:T(8,128)S(1)} %maximum_convert_fusion, f32[1536]{0:T(1024)S(1)} %get-tuple-element.76, f32[1536]{0:T(1024)S(1)} %get-tuple-element.77, f32[1536]{0:T(1024)S(1)} %get-tuple-element.47, f32[1536]{0:T(1024)S(1)} %get-tuple-element.48, ...), kind=kLoop, calls=%fused_computation.264 | loop fusion | flops 37747200 | bytes 78059520 | tf_op jit(solution)/shard_map/reduce_sum | solution.py:51
  150.5 44.4 %psum.56 = f32[1536]{0:T(1024)S(1)} all-reduce(f32[1536]{0:T(1024)S(1)} %get-tuple-element.85), channel_id=1, replica_groups=mesh['seq'=8,'fsdp'=4] {'seq','fsdp'}, use_global_device_ids=true, to_apply=%region_3.4 | all-reduce | flops 1536 | bytes 12288 | tf_op jit(solution)/shard_map/psum | solution.py:51
  196.8 40.4 %psum.57 = f32[1536]{0:T(1024)S(1)} all-reduce(f32[1536]{0:T(1024)S(1)} %multiply_reduce_fusion.33), channel_id=1, replica_groups=mesh['seq'=8,'fsdp'=4] {'seq','fsdp'}, use_global_device_ids=true, to_apply=%region_5.6 | all-reduce | flops 1536 | bytes 12288 | tf_op jit(solution)/shard_map/psum | solution.py:53
  237.2 4.5 fusion.118
  241.7 40.0 %all-reduce.1 = (f32[1536]{0:T(1024)S(1)}, f32[1536]{0:T(1024)S(1)}) all-reduce(f32[1536]{0:T(1024)S(1)} %get-tuple-element.41, f32[1536]{0:T(1024)S(1)} %get-tuple-element.40), channel_id=1, replica_groups=mesh['seq'=8,'fsdp'=4] {'seq','fsdp'}, use_global_device_ids=true, to_apply=%region_9.10 | all-reduce | flops 3072 | bytes 24576 | tf_op jit(solution)/shard_map/psum | solution.py:60
  282.3 8.2 %multiply_reduce_fusion = (f32[1536]{0:T(1024)S(1)}, f32[1536]{0:T(1024)S(1)}, f32[1536]{0:T(1024)S(1)}, f32[1536]{0:T(1024)S(1)}, f32[1536]{0:T(1024)S(1)}, /*i...) fusion(f32[415,1536]{1,0:T(8,128)S(1)} %maximum_convert_fusion,, ...), kind=kLoop, calls=%fused_computation.171 | loop fusion | flops 31822848 | bytes 48519168 | tf_op jit(solution)/shard_map/reduce_sum | solution.py:73
  293.4 2.0 collective-permute-done.3
  295.4 42.4 %multiply_convert_fusion.1 = (bf16[384,1536]{1,0:T(8,128)(2,1)S(1)}, f32[384,1536]{1,0:T(8,128)}) fusion(f32[384,3072]{1,0:T(8,128)} %copy-done, f32[31,1536]{1,0:T(8,128)S(1)} %collective-permute-done.3, f32[384,1536]{1,0:T(8,128)} %copy-done.1, f32[1536]{0:T(1024)S(1)} %get-tuple-element.76, f32[1536]{0:T(1024)S(1)} %get-tuple-element.77, ...), kind=kLoop, calls=%fused_computation.204 | loop fusion | flops 58392576 | bytes 8644608 | tf_op jit(solution)/shard_map/convert
  337.8 4.4 multiply_convert_fusion
  343.3 9.4 %fusion.111 = f32[1536,3072]{1,0:T(8,128)} fusion(bf16[384,1536]{1,0:T(8,128)(2,1)S(1)} %multiply_convert_fusion, bf16[384,1536]{1,0:T(8,128)(2,1)S(1)} %get-tuple-element.83, bf16[384,1536]{1,0:T(8,128)(2,1)S(1)} %copy-done.3, f32[1536]{0:T(1024)S(1)} %copy-done.11, f32[1536]{0:T(1024)S(1)} %copy-done.10, f32[384]{0:T(512)S(1)} %add_rsqrt_fusion.1, ...), kind=kOutput, calls=%fused_computation.218 | convolution fusion | flops 3632136192 | bytes 22428672 | tf_op jit(solution)/shard_map/dot_general | solution.py:101
  352.8 5.4 multiply_reduce_fusion.18
  358.7 2.8 stack.131
  361.7 135.2 %reduce-scatter.2.cloned.1.call-done = f32[384,3072]{1,0:T(8,128)} async-done(((f32[1536,3072]{1,0:T(8,128)}), f32[384,3072]{1,0:T(8,128)}) %reduce-scatter.2.cloned.1.call-update) | async-done | bytes 4718608 | tf_op jit(solution)/shard_map/reduce_scatter | solution.py:100
  498.9 12.5 %fusion.12 = (f32[1536]{0:T(1024)}, f32[384]{0:T(512)}, f32[384]{0:T(512)}, f32[1536]{0:T(1024)}, f32[384,1536]{1,0:T(8,128)}) fusion(bf16[384,1536]{1,0:T(8,128)(2,1)S(1)} %copy-done.4, f32[384]{0:T(512)S(1)} %add_rsqrt_fusion.1, f32[384]{0:T(512)S(1)} %broadcast_multiply_fusion.4, f32[1536]{0:T(1024)S(1)} %copy-done.10, ...), kind=kOutput, calls=%fused_computation.46 | convolution fusion | flops 3676958720 | bytes 15360001 | tf_op jit(solution)/shard_map/dot_general | solution.py:83
  511.5 39.6 %all-reduce = (f32[1536]{0:T(1024)}, f32[1536]{0:T(1024)}) all-reduce(f32[1536]{0:T(1024)} %get-tuple-element.42, f32[1536]{0:T(1024)} %get-tuple-element.45), channel_id=1, replica_groups=mesh['seq'=8,'fsdp'=4] {'seq','fsdp'}, use_global_device_ids=true, to_apply=%region_48.49 | all-reduce | flops 3072 | bytes 24576 | tf_op jit(solution)/shard_map/psum | solution.py:86
  551.8 3.4 fusion.11
  555.2 165.7 %all-reduce.5.cloned.1.call-done = f32[384,3072]{1,0:T(8,128)} async-done(((f32[384,3072]{1,0:T(8,128)}), f32[384,3072]{1,0:T(8,128)}) %all-reduce.5.cloned.1.call-update) | async-done | bytes 4718608 | tf_op jit(solution)/shard_map/psum | solution.py:111
  721.0 5.1 copy.18
  (90 shorter events, 17.2 us)
Async XLA Ops:
  8.0 488.9 %reduce-scatter.2.cloned.1.call-start = ((), (), s32[]{:S(2)}) async-start(), calls=%async_computation.1 | async-start | bytes 23592960 | tf_op jit(solution)/shard_map/reduce_scatter | solution.py:100
  8.0 4.9 collective-permute-start
  8.6 15.9 %copy-start.2 = (bf16[384,1536]{1,0:T(8,128)(2,1)S(1)}, bf16[384,1536]{1,0:T(8,128)(2,1)}, u32[]{:S(2)}) copy-start(bf16[384,1536]{1,0:T(8,128)(2,1)} %param.8) | copy-start | bytes 3538948
  19.6 105.3 %copy-start.10 = (f32[1536]{0:T(1024)S(1)}, f32[1536]{0:T(1024)}, u32[]{:S(2)}) copy-start(f32[1536]{0:T(1024)} %param.9) | copy-start | bytes 18436
  19.6 105.3 %copy-start.11 = (f32[1536]{0:T(1024)S(1)}, f32[1536]{0:T(1024)}, u32[]{:S(2)}) copy-start(f32[1536]{0:T(1024)} %param.10) | copy-start | bytes 18436
  19.6 105.3 %collective-permute-start.1 = (bf16[768,3072]{1,0:T(8,128)(2,1)}, bf16[768,3072]{1,0:T(8,128)(2,1)}, u32[]{:S(2)}, u32[]{:S(2)}) collective-permute-start(bf16[768,3072]{1,0:T(8,128)(2,1)} %maximum_select_fusion.1), channel_id=1, source_target_pairs={{0,2},{1,3},{2,0},{3,1},{4,6},{5,7},{6,4},{7,5},{8,10},{9,11},{10,... | collective-permute-start | bytes 14155784 | tf_op jit(solution)/shard_map/ppermute | solution.py:33
  134.6 2.1 copy-start
  136.7 3.2 collective-permute-start.2
  150.5 86.7 %copy-start.12 = (f32[1536]{0:T(1024)S(1)}, f32[1536]{0:T(1024)}, u32[]{:S(2)}) copy-start(f32[1536]{0:T(1024)} %param.13) | copy-start | bytes 18436
  150.5 86.8 %copy-start.13 = (f32[1536]{0:T(1024)S(1)}, f32[1536]{0:T(1024)}, u32[]{:S(2)}) copy-start(f32[1536]{0:T(1024)} %param.14) | copy-start | bytes 18436
  281.7 0.6 copy-start.15
  281.7 8.9 %copy-start.14 = (f32[1536]{0:T(1024)}, f32[1536]{0:T(1024)S(1)}, u32[]{:S(2)}) copy-start(f32[1536]{0:T(1024)S(1)} %get-tuple-element.97) | copy-start | bytes 18436
  290.6 1.5 copy-start.1
  292.1 3.3 collective-permute-start.3
  337.8 4.5 copy-start.5
  337.8 5.5 copy-start.3
  342.3 1.0 copy-start.7
  352.7 202.5 %all-reduce.7.cloned.1.call-start = ((), (), s32[]{:S(2)}) async-start(), calls=%async_computation.3 | async-start | bytes 393216 | tf_op jit(solution)/shard_map/psum | solution.py:86
  361.5 359.5 %all-reduce.5.cloned.1.call-start = ((), (), s32[]{:S(2)}) async-start(), calls=%async_computation.2 | async-start | bytes 9437184 | tf_op jit(solution)/shard_map/psum | solution.py:111
  496.9 1.3 copy-start.4
  496.9 1.6 copy-start.6
  496.9 2.0 copy-start.8
  721.0 5.1 copy-start.9
Sparse Core Ops, SparseCore 0:
  352.8 144.0 reduce-scatter.1
Sparse Core Ops, SparseCore 1:
  361.5 185.3 all-reduce.6
  550.8 170.1 all-reduce.4
